TPU v7x, 512 devices: a whole 4x4x16 slice. The times are simulated.
512 devices in a mesh: mpo: 16 (over z), sec: 32 (over x, y, core).
Axes of the slice: x: 4, y: 4, z: 16, core: 2. Of those that a mesh axis runs over, the one named last changes fastest.
Arguments:
- environment: bfloat16 [48, 64, 128, 128], P('mpo', 'sec'), may hold values from -6 to 6
- site_tensor: bfloat16 [64, 4, 128, 128], P('sec'), may hold values from -0.25 to 0.25
- mpo_tensor: bfloat16 [48, 48, 4, 4], P('mpo'), may hold values from -0.75 to 0.75
- mpo_pattern: int32 [48, 48], P('mpo'), may hold values 0 or 1
- sector_rows: int32 [64], replicated, may hold values from 64 to 128
- sector_map: int32 [64], replicated, may hold values from 0 to 63, as said below
Outputs:
- new_environment: bfloat16 [48, 64, 128, 128], P('mpo', 'sec')
Inputs may be any that keep to these rules, and one draw needn't show every extreme that they name: A permutation of the 64 sector labels: sector g takes the new label sector_map[g].
All inputs are finite; a program needn't handle non-finite values. No bound on the sum of `mpo_pattern` on one device may be relied on, other than what follows from the above.
Results may differ from a plain program's by a relative error of at most 0.02.
Values may be sent and summed in bfloat16 or wider, within the bound.
No kernel may reach another device: no remote copies, remote signals or barrier semaphores. Data moves between devices by JAX's collectives and lax.ppermute only.
A program may use at most 64 MiB of HBM per device.

v0:
```python
import jax
import jax.numpy as jnp
from jax import lax
from jax.sharding import PartitionSpec as P


def attach_site(env_block, site_tensor):
    return jnp.einsum(
        "bgac,gtcz->gbtaz", env_block, site_tensor, preferred_element_type=jnp.float32
    ).astype(jnp.bfloat16)


def mix_project(attached, weight_block, site_tensor):
    mixed = jnp.einsum(
        "bpst,gbtaz->gpsaz", weight_block, attached, preferred_element_type=jnp.float32
    ).astype(jnp.bfloat16)
    return jnp.einsum("gsxa,gpsxz->pgaz", site_tensor, mixed, preferred_element_type=jnp.float32)


def per_device(environment, site_tensor, mpo_tensor, mpo_pattern, sector_rows, sector_map):
    channels = environment.shape[0]
    per_dev = environment.shape[1]
    block = environment.shape[2]
    masked = jnp.where(mpo_pattern[:, :, None, None] != 0, mpo_tensor, jnp.zeros_like(mpo_tensor))
    attached = attach_site(environment, site_tensor)

    def one_block(offset):
        weight_block = lax.dynamic_slice_in_dim(masked, offset * channels, channels, 1)
        return mix_project(attached, weight_block, site_tensor)

    parts = lax.map(
        one_block, jnp.arange(channels * lax.axis_size("mpo") // channels, dtype=jnp.int32)
    )
    summed = lax.psum_scatter(
        parts.reshape(channels * lax.axis_size("mpo"), per_dev, block, block).astype(jnp.bfloat16),
        "mpo",
        scatter_dimension=0,
        tiled=True,
    )
    result = summed
    ranks = lax.axis_size("sec")
    device = lax.axis_index("sec")
    local = jnp.arange(per_dev, dtype=jnp.int32)
    own_labels = device * per_dev + local
    sizes = jnp.take(sector_rows, own_labels, axis=0)
    places = jnp.arange(block, dtype=jnp.int32)
    keep = (places[None, :, None] < sizes[:, None, None]) & (
        places[None, None, :] < sizes[:, None, None]
    )
    result = jnp.where(keep[None, :, :, :], result, jnp.zeros_like(result))
    target = jnp.take(sector_map, own_labels, axis=0)
    owner = target // per_dev
    place = target % per_dev
    owners = jnp.arange(ranks, dtype=jnp.int32)
    onehot = (owners[:, None, None] == owner[None, None, :]) & (
        local[None, :, None] == place[None, None, :]
    )
    outgoing = jnp.einsum(
        "nuj,cjab->ncuab", onehot.astype(jnp.bfloat16), result, preferred_element_type=jnp.float32
    ).astype(jnp.bfloat16)
    received = lax.all_to_all(outgoing, "sec", split_axis=0, concat_axis=0, tiled=True)
    return jnp.sum(received, axis=0, dtype=jnp.float32).astype(jnp.bfloat16)


def solution(mesh):
    return jax.shard_map(
        per_device,
        mesh=mesh,
        in_specs=(
            P("mpo", "sec", None, None),
            P("sec", None, None, None),
            P("mpo", None, None, None),
            P("mpo", None),
            P(),
            P(),
        ),
        out_specs=P("mpo", "sec", None, None),
        check_vma=False,
    )
```

profile of v0, /device:TPU:1, one launch (start us, length us, event | category | flops | bytes accessed | tf_op | source)
XLA Modules:
  0.0 264.2 jit_solution(16546818520940792293)
XLA Ops:
  6.5 0.7 broadcast_compare_fusion
  7.3 0.9 copy.17
  8.2 1.4 fusion.7
  10.2 62.2 %while.10 = (s32[]{:T(128)}, bf16[16,3,2,128,128]{4,3,2,1,0:T(8,128)(2,1)}, s32[16]{0:T(128)S(1)}, bf16[3,48,4,4]{3,1,0,2:T(8,128)(2,1)S(1)}, bf16[2,3,4,128,128...) while((s32[]{:T(128)}, ...), condition=%wide.region_1.3_spmd, body=%wide.region_0.2_spmd.sunk | while | flops 110493704 | bytes 3616943 | solution.py:31
  11.3 1.5 fusion.25
  15.2 1.5 fusion.25
  17.3 0.7 constant_dynamic-update-slice_fusion.2
  19.1 1.5 fusion.25
  23.0 1.5 fusion.25
  26.9 1.5 fusion.25
  30.8 1.5 fusion.25
  32.8 0.7 constant_dynamic-update-slice_fusion.2
  34.6 1.5 fusion.25
  38.5 1.5 fusion.25
  40.6 0.7 constant_dynamic-update-slice_fusion.2
  42.4 1.5 fusion.25
  46.3 1.5 fusion.25
  50.2 1.5 fusion.25
  54.1 1.5 fusion.25
  56.1 0.7 constant_dynamic-update-slice_fusion.2
  58.0 1.5 fusion.25
  61.9 1.5 fusion.25
  65.7 1.5 fusion.25
  69.6 1.5 fusion.25
  71.7 0.7 constant_dynamic-update-slice_fusion.2
  74.6 71.1 %reduce-scatter.2.cloned.1.call-done = bf16[3,2,128,128]{3,2,1,0:T(8,128)(2,1)} async-done(((bf16[48,2,128,128]{3,2,1,0:T(8,128)(2,1)}), bf16[3,2,128,128]{3,2,1,0:T(8,128)(2,1)}) %reduce-scatter.2.cloned.1.call-update) | async-done | bytes 196624 | tf_op jit(solution)/shard_map/reduce_scatter | solution.py:34
  145.7 0.9 select_bitcast_fusion
  146.7 1.9 convert_bitcast_fusion
  148.6 8.7 %copy.23 = bf16[32,3,2,128,128]{4,2,3,1,0:T(2,128)(2,1)S(1)} copy(bf16[32,3,2,128,128]{4,0,2,3,1:T(8,128)(2,1)S(1)} %convert_bitcast_fusion) | data formatting | bytes 12582912 | tf_op jit(solution)/shard_map/convert_element_type | solution.py:60
  157.3 89.7 %all_to_all.5 = bf16[32,3,2,128,128]{4,2,3,1,0:T(2,128)(2,1)} all-to-all(bf16[32,3,2,128,128]{4,2,3,1,0:T(2,128)(2,1)S(1)} %copy.23), channel_id=1, replica_groups=mesh['mpo'=16,'sec'=32] {'sec'}, dimensions={0} | all-to-all | bytes 12582912 | tf_op jit(solution)/shard_map/all_to_all | solution.py:61
  246.9 9.7 %reduce_sum.12 = bf16[3,2,128,128]{3,1,2,0:T(2,128)(2,1)S(1)} reduce(bf16[32,3,2,128,128]{4,2,3,1,0:T(2,128)(2,1)} %all_to_all.5, bf16[]{:T(256)} %constant.59.clone.1), dimensions={0}, to_apply=%region_3.5 | reduce | flops 3047424 | bytes 6488066 | tf_op jit(solution)/shard_map/reduce_sum | solution.py:62
  256.6 0.7 copy.25
  (83 shorter events, 29.0 us)
Async XLA Ops:
  6.5 1.6 copy-start
  6.5 3.7 %copy-start.3 = (bf16[2,4,128,128]{3,2,1,0:T(8,128)(2,1)S(1)}, bf16[2,4,128,128]{3,2,1,0:T(8,128)(2,1)}, u32[]{:S(2)}) copy-start(bf16[2,4,128,128]{3,2,1,0:T(8,128)(2,1)} %param.11) | copy-start | bytes 786436
  6.5 139.2 %reduce-scatter.2.cloned.1.call-start = ((), (), s32[]{:S(2)}) async-start(), calls=%async_computation.2 | async-start | bytes 3342336 | tf_op jit(solution)/shard_map/reduce_scatter | solution.py:34
  72.4 0.7 copy-start.1
  72.4 1.3 copy-start.2
Sparse Core Ops, SparseCore 0:
  72.5 73.1 reduce-scatter.1
where the time goes:
time: 265 us; the launch traced here: 264 us
  blocking collectives  89.7 us (34%)
  waiting for transfers between devices  71.1 us (27%)
  local copies, waits for them, and re-layouts  35.5 us (13%)
  matrix products  33.6 us (13%)
  between operations  13.5 us (5%)
  other arithmetic  11.8 us (4%)
  loops' own time  9.09 us (3%)
    all_to_all x1, blocking collectives, per_device(): lax.all_to_all(outgoing, 'sec', split_axis=0, concat_axis=0, tiled=True)  89.7 us
    reduce_scatter x1, waiting for transfers between devices, per_device(): lax.psum_scatter(parts.reshape(channels * lax.axis_size('mpo'), per_dev,...  71.1 us
    dot_general x16, matrix products, mix_project(): jnp.einsum('bpst,gbtaz->gpsaz', weight_block, attached, preferred_element...  23.4 us
    dynamic_update_slice x32, local copies, waits for them, and re-layouts, per_device(): lax.map(one_block, jnp.arange(channels * lax.axis_size('mpo') // channels...  13.9 us
    reduce_sum x1, other arithmetic, per_device(): return jnp.sum(received, axis=0, dtype=jnp.float32).astype(jnp.bfloat16)  9.7 us
    another operation x1, loops' own time, per_device(): lax.map(one_block, jnp.arange(channels * lax.axis_size('mpo') // channels...  9.09 us
    dynamic_slice x16, local copies, waits for them, and re-layouts, per_device(): lax.map(one_block, jnp.arange(channels * lax.axis_size('mpo') // channels...  8.87 us
    convert_element_type x1, local copies, waits for them, and re-layouts, per_device(): outgoing = jnp.einsum('nuj,cjab->ncuab', onehot.astype(jnp.bfloat16), res...  8.69 us
  transfers between devices with their start and end apart: 1, of which 1 were waited for; matrix products, arithmetic and copies ran while one was open for 1% of the time, Pallas kernels for 0%

commit v1 on v0

v1 whole, which is shorter than its diff:
```python
import jax
import jax.numpy as jnp
from jax import lax
from jax.sharding import PartitionSpec as P


def per_device(environment, site_tensor, mpo_tensor, mpo_pattern, sector_rows, sector_map):
    per_dev = environment.shape[1]
    block = environment.shape[2]
    masked = jnp.where(mpo_pattern[:, :, None, None] != 0, mpo_tensor, jnp.zeros_like(mpo_tensor))
    left = jnp.einsum(
        "gsxa,bgxc->gbsac", site_tensor, environment, preferred_element_type=jnp.float32
    ).astype(jnp.bfloat16)
    sandwich = jnp.einsum(
        "gbsac,gtcz->bstgaz", left, site_tensor, preferred_element_type=jnp.float32
    ).astype(jnp.bfloat16)
    parts = jnp.einsum(
        "bpst,bstgaz->pgaz", masked, sandwich, preferred_element_type=jnp.float32
    ).astype(jnp.bfloat16)
    summed = lax.psum_scatter(parts, "mpo", scatter_dimension=0, tiled=True)
    device = lax.axis_index("sec")
    local = jnp.arange(per_dev, dtype=jnp.int32)
    own_labels = device * per_dev + local
    sizes = jnp.take(sector_rows, own_labels, axis=0)
    places = jnp.arange(block, dtype=jnp.int32)
    keep = (places[None, :, None] < sizes[:, None, None]) & (
        places[None, None, :] < sizes[:, None, None]
    )
    result = jnp.where(keep[None, :, :, :], summed, jnp.zeros_like(summed))
    gathered = lax.all_gather(result, "sec", axis=1, tiled=True)
    nsec = sector_map.shape[0]
    inverse = jnp.zeros((nsec,), jnp.int32).at[sector_map].set(jnp.arange(nsec, dtype=jnp.int32))
    source = jnp.take(inverse, own_labels, axis=0)
    return jnp.take(gathered, source, axis=1)


def solution(mesh):
    return jax.shard_map(
        per_device,
        mesh=mesh,
        in_specs=(
            P("mpo", "sec", None, None),
            P("sec", None, None, None),
            P("mpo", None, None, None),
            P("mpo", None),
            P(),
            P(),
        ),
        out_specs=P("mpo", "sec", None, None),
        check_vma=False,
    )
```

time: 265 us -> 175 us (0.66)
  blocking collectives: 89.7 us -> 0 us
  waiting for transfers between devices: 71.1 us -> 143 us
  matrix products: 33.6 us -> 6.18 us
  local copies, waits for them, and re-layouts: 35.5 us -> 10.1 us
  other arithmetic: 11.8 us -> 1.98 us
  loops' own time: 9.09 us -> 0 us
    all_to_all x1 -> x0, blocking collectives: 89.7 us -> none  [per_device(): lax.all_to_all(outgoing, 'sec', split_axis=0, concat_axis=0, tiled=True)]
    all_gather x0 -> x1, waiting for transfers between devices: none -> 71.5 us  [per_device(): gathered = lax.all_gather(result, 'sec', axis=1, tiled=True)]
    dot_general x34 -> x2, matrix products: 33.6 us -> 6.18 us  [the longest x1 4.03 us: per_device(): jnp.einsum('bpst,bstgaz->pgaz', masked, sandwich, preferred_element_type=...]
    dynamic_update_slice x32 -> x0, local copies, waits for them, and re-layouts: 13.9 us -> none  [per_device(): lax.map(one_block, jnp.arange(channels * lax.axis_size('mpo') // channels...]
    reduce_sum x1 -> x0, other arithmetic: 9.7 us -> none  [per_device(): return jnp.sum(received, axis=0, dtype=jnp.float32).astype(jnp.bfloat16)]
    another operation x1 -> x0, loops' own time: 9.09 us -> none  [per_device(): lax.map(one_block, jnp.arange(channels * lax.axis_size('mpo') // channels...]
    dynamic_slice x16 -> x0, local copies, waits for them, and re-layouts: 8.87 us -> none  [per_device(): lax.map(one_block, jnp.arange(channels * lax.axis_size('mpo') // channels...]
    convert_element_type x1, local copies, waits for them, and re-layouts: 8.69 us -> 2.48 us  [per_device(): parts = jnp.einsum('bpst,bstgaz->pgaz', masked, sandwich, preferred_eleme...]
  transfers between devices with their start and end apart: 1 -> 2, of which waited for: 1 -> 2; matrix products, arithmetic and copies ran while one was open for 1% -> 1% of each run, Pallas kernels for 0% -> 0%
where the time goes in v1:
time: 175 us
  waiting for transfers between devices  143 us (82%)
  between operations  13.5 us (8%)
  local copies, waits for them, and re-layouts  10.1 us (6%)
  matrix products  6.18 us (4%)
  other arithmetic  1.98 us (1%)
    reduce_scatter x1, waiting for transfers between devices, per_device(): summed = lax.psum_scatter(parts, 'mpo', scatter_dimension=0, tiled=True)  71.9 us
    all_gather x1, waiting for transfers between devices, per_device(): gathered = lax.all_gather(result, 'sec', axis=1, tiled=True)  71.5 us
    dot_general x1, matrix products, per_device(): jnp.einsum('bpst,bstgaz->pgaz', masked, sandwich, preferred_element_type=...  4.03 us
  transfers between devices with their start and end apart: 2, of which 2 were waited for; matrix products, arithmetic and copies ran while one was open for 1% of the time, Pallas kernels for 0%

profile of v1, /device:TPU:1, one launch (start us, length us, event | category | flops | bytes accessed | tf_op | source)
XLA Modules:
  0.0 175.2 jit_solution(12927616610973831131)
XLA Ops:
  6.5 0.0 copy-start
  6.5 0.0 copy-start.2
  6.5 0.0 reduce-scatter.2.cloned.1.call-start
  6.5 0.7 broadcast_compare_fusion
  7.3 0.2 copy-done
  7.5 2.1 %convert_bitcast_fusion = bf16[3,4,4,2,128,128]{5,4,2,1,0,3:T(8,128)(2,1)S(1)} fusion(bf16[2,4,128,128]{3,2,1,0:T(8,128)(2,1)S(1)} %copy-done, bf16[3,2,128,128]{3,2,1,0:T(8,128)(2,1)} %param.8), kind=kOutput, calls=%fused_computation.7 | convolution fusion | flops 505282560 | bytes 3604480 | tf_op jit(solution)/shard_map/gbsac,gtcz->bstgaz/dot_general | solution.py:14
  9.7 0.0 copy-done.2
  9.7 4.0 %bitcast_convert_fusion = bf16[48,2,128,128]{3,0,2,1:T(8,128)(2,1)S(1)} fusion(bf16[3,4,4,2,128,128]{5,4,2,1,0,3:T(8,128)(2,1)S(1)} %convert_bitcast_fusion, bf16[3,48,4,4]{1,3,2,0:T(4,128)(2,1)S(1)} %copy-done.2, pred[3,48]{1,0:T(4,128)(4,1)S(1)} %broadcast_compare_fusion), kind=kOutput, calls=%fused_computation.4 | convolution fusion | flops 152570112 | bytes 6296208 | tf_op jit(solution)/shard_map/bpst,bstgaz->pgaz/dot_general | solution.py:17
  13.7 2.5 %copy.12 = bf16[48,2,128,128]{3,2,1,0:T(8,128)(2,1)} copy(bf16[48,2,128,128]{3,0,2,1:T(8,128)(2,1)S(1)} %bitcast_convert_fusion) | data formatting | bytes 6291456 | tf_op jit(solution)/shard_map/convert_element_type | solution.py:19
  16.2 0.0 copy-start.1
  16.2 0.0 copy-start.3
  16.2 0.0 reduce-scatter.2.cloned.1.call-update
  16.2 0.0 all-gather.2.cloned.1.call-start
  16.3 0.5 copy-done.1
  16.8 0.6 gather_fusion.2
  17.5 0.1 iota_compare_fusion
  17.6 0.1 broadcast_and_fusion
  17.7 71.9 %reduce-scatter.2.cloned.1.call-done = bf16[3,2,128,128]{3,2,1,0:T(8,128)(2,1)} async-done(((bf16[48,2,128,128]{3,2,1,0:T(8,128)(2,1)}), bf16[3,2,128,128]{3,2,1,0:T(8,128)(2,1)}) %reduce-scatter.2.cloned.1.call-update) | async-done | bytes 196624 | tf_op jit(solution)/shard_map/reduce_scatter | solution.py:20
  89.6 0.9 broadcast_select_fusion
  90.5 0.7 copy.13
  91.2 0.0 all-gather.2.cloned.1.call-update
  91.3 0.0 copy-done.3
  91.3 0.8 scatter_custom_fusion
  92.1 0.6 gather_fusion.1
  92.7 71.5 %all-gather.2.cloned.1.call-done = bf16[3,64,128,128]{3,2,0,1:T(8,128)(2,1)} async-done(((bf16[3,2,128,128]{3,2,0,1:T(8,128)(2,1)}), bf16[3,64,128,128]{3,2,0,1:T(8,128)(2,1)}) %all-gather.2.cloned.1.call-update) | async-done | bytes 6291472 | tf_op jit(solution)/shard_map/all_gather | solution.py:30
  164.2 3.4 %gather_fusion = bf16[2,3,128,128]{3,2,1,0:T(8,128)(2,1)S(1)} fusion(bf16[3,64,128,128]{3,2,0,1:T(8,128)(2,1)} %all-gather.2.cloned.1.call-done, s32[1024]{0:T(1024)S(1)} %pad_clamp_fusion), kind=kCustom, calls=%fused_computation.2 | custom fusion | bytes 393224 | tf_op jit(solution)/shard_map/jit(_take)/gather | solution.py:34
  167.6 0.1 select_bitcast_fusion
  167.7 0.7 copy.14
  (7 shorter events, 0.0 us)
Async XLA Ops:
  6.5 1.0 copy-start
  6.5 3.1 %copy-start.2 = (bf16[3,48,4,4]{1,3,2,0:T(4,128)(2,1)S(1)}, bf16[3,48,4,4]{1,3,2,0:T(4,128)(2,1)}, u32[]{:S(2)}) copy-start(bf16[3,48,4,4]{1,3,2,0:T(4,128)(2,1)} %param.10) | copy-start | bytes 13828
  6.5 83.1 %reduce-scatter.2.cloned.1.call-start = ((), (), s32[]{:S(2)}) async-start(), calls=%async_computation.1 | async-start | bytes 3342336 | tf_op jit(solution)/shard_map/reduce_scatter | solution.py:20
  16.2 0.7 copy-start.1
  16.2 75.1 %copy-start.3 = (s32[64]{0:T(128)S(1)}, s32[64]{0:T(128)}, u32[]{:S(2)}) copy-start(s32[64]{0:T(128)} %param.13) | copy-start | bytes 772
  16.2 148.0 %all-gather.2.cloned.1.call-start = ((), (), s32[]{:S(2)}) async-start(), calls=%async_computation.2 | async-start | bytes 6488064 | tf_op jit(solution)/shard_map/all_gather | solution.py:30
Sparse Core Ops, SparseCore 0:
  16.3 73.2 reduce-scatter.1
  92.7 71.4 all-gather.1

commit v2 on v1

v2 whole, which is shorter than its diff:
```python
import jax
import jax.numpy as jnp
from jax import lax
from jax.sharding import PartitionSpec as P


def per_device(environment, site_tensor, mpo_tensor, mpo_pattern, sector_rows, sector_map):
    channels, per_dev, block = environment.shape[0], environment.shape[1], environment.shape[2]
    nsec = sector_map.shape[0]
    device = lax.axis_index("sec")
    local = jnp.arange(per_dev, dtype=jnp.int32)
    own_labels = device * per_dev + local
    inverse = jnp.zeros((nsec,), jnp.int32).at[sector_map].set(jnp.arange(nsec, dtype=jnp.int32))
    source = jnp.take(inverse, own_labels, axis=0)
    sizes = jnp.take(sector_rows, source, axis=0)

    masked = jnp.where(mpo_pattern[:, :, None, None] != 0, mpo_tensor, jnp.zeros_like(mpo_tensor))
    left = jnp.einsum(
        "gsxa,bgxc->gbsac", site_tensor, environment, preferred_element_type=jnp.float32
    ).astype(jnp.bfloat16)
    sandwich = jnp.einsum(
        "gbsac,gtcz->bstgaz", left, site_tensor, preferred_element_type=jnp.float32
    ).astype(jnp.bfloat16)
    parts = jnp.einsum(
        "bpst,bstgaz->pgaz", masked, sandwich, preferred_element_type=jnp.float32
    ).astype(jnp.bfloat16)
    summed = lax.psum_scatter(parts, "mpo", scatter_dimension=0, tiled=True)
    gathered = lax.all_gather(summed, "sec", axis=1, tiled=True)
    places = jnp.arange(block, dtype=jnp.int32)
    picked = []
    for k in range(per_dev):
        one = lax.dynamic_index_in_dim(gathered, source[k], axis=1, keepdims=False)
        keep = (places[:, None] < sizes[k]) & (places[None, :] < sizes[k])
        picked.append(jnp.where(keep[None], one, jnp.zeros_like(one)))
    return jnp.stack(picked, axis=1)


def solution(mesh):
    return jax.shard_map(
        per_device,
        mesh=mesh,
        in_specs=(
            P("mpo", "sec", None, None),
            P("sec", None, None, None),
            P("mpo", None, None, None),
            P("mpo", None),
            P(),
            P(),
        ),
        out_specs=P("mpo", "sec", None, None),
        check_vma=False,
    )
```

time: 175 us -> 173 us (0.989)
  waiting for transfers between devices: 143 us -> 138 us
  between operations: 13.5 us -> 17.3 us
    all_gather x1, waiting for transfers between devices: 71.5 us -> 64 us  [per_device(): gathered = lax.all_gather(summed, 'sec', axis=1, tiled=True)]
    gather x2 -> x1, local copies, waits for them, and re-layouts: 4 us -> 0.64 us  [per_device(): sizes = jnp.take(sector_rows, source, axis=0)]
  transfers between devices with their start and end apart: 2 -> 2, of which waited for: 2 -> 2; matrix products, arithmetic and copies ran while one was open for 1% -> 3% of each run, Pallas kernels for 0% -> 0%
where the time goes in v2:
time: 173 us
  waiting for transfers between devices  138 us (80%)
  between operations  17.3 us (10%)
  local copies, waits for them, and re-layouts  8.36 us (5%)
  matrix products  6.29 us (4%)
  other arithmetic  3.12 us (2%)
    reduce_scatter x1, waiting for transfers between devices, per_device(): summed = lax.psum_scatter(parts, 'mpo', scatter_dimension=0, tiled=True)  73.6 us
    all_gather x1, waiting for transfers between devices, per_device(): gathered = lax.all_gather(summed, 'sec', axis=1, tiled=True)  64 us
    dot_general x1, matrix products, per_device(): jnp.einsum('bpst,bstgaz->pgaz', masked, sandwich, preferred_element_type=...  4.14 us
  transfers between devices with their start and end apart: 2, of which 2 were waited for; matrix products, arithmetic and copies ran while one was open for 3% of the time, Pallas kernels for 0%

profile of v2, /device:TPU:1, one launch (start us, length us, event | category | flops | bytes accessed | tf_op | source)
XLA Modules:
  0.0 172.8 jit_solution(9636265486382752984)
XLA Ops:
  6.5 0.0 copy-start
  6.5 0.0 copy-start.2
  6.5 0.0 reduce-scatter.2.cloned.1.call-start
  6.5 0.7 broadcast_compare_fusion
  7.3 0.2 copy-done
  7.5 2.1 %convert_bitcast_fusion = bf16[3,4,4,2,128,128]{5,4,2,1,0,3:T(8,128)(2,1)S(1)} fusion(bf16[2,4,128,128]{3,2,1,0:T(8,128)(2,1)S(1)} %copy-done, bf16[3,2,128,128]{3,2,1,0:T(8,128)(2,1)} %param.8), kind=kOutput, calls=%fused_computation.6 | convolution fusion | flops 505282560 | bytes 3604480 | tf_op jit(solution)/shard_map/gbsac,gtcz->bstgaz/dot_general | solution.py:21
  9.7 0.0 copy-done.2
  9.7 4.1 %bitcast_convert_fusion = bf16[48,2,128,128]{3,0,2,1:T(8,128)(2,1)S(1)} fusion(bf16[3,4,4,2,128,128]{5,4,2,1,0,3:T(8,128)(2,1)S(1)} %convert_bitcast_fusion, bf16[3,48,4,4]{1,3,2,0:T(4,128)(2,1)S(1)} %copy-done.2, pred[3,48]{1,0:T(4,128)(4,1)S(1)} %broadcast_compare_fusion), kind=kOutput, calls=%fused_computation.3 | convolution fusion | flops 152570112 | bytes 6296208 | tf_op jit(solution)/shard_map/bpst,bstgaz->pgaz/dot_general | solution.py:24
  13.8 2.5 %copy.12 = bf16[48,2,128,128]{3,2,1,0:T(8,128)(2,1)} copy(bf16[48,2,128,128]{3,0,2,1:T(8,128)(2,1)S(1)} %bitcast_convert_fusion) | data formatting | bytes 6291456 | tf_op jit(solution)/shard_map/convert_element_type | solution.py:26
  16.3 0.0 copy-start.3
  16.3 0.0 copy-start.1
  16.3 0.0 reduce-scatter.2.cloned.1.call-update
  16.3 0.0 all-gather.2.cloned.1.call-start
  16.4 73.6 %reduce-scatter.2.cloned.1.call-done = bf16[3,2,128,128]{3,2,1,0:T(8,128)(2,1)} async-done(((bf16[48,2,128,128]{3,2,1,0:T(8,128)(2,1)}), bf16[3,2,128,128]{3,2,1,0:T(8,128)(2,1)}) %reduce-scatter.2.cloned.1.call-update) | async-done | bytes 196624 | tf_op jit(solution)/shard_map/reduce_scatter | solution.py:27
  90.0 1.6 copy.13
  91.6 0.0 all-gather.2.cloned.1.call-update
  91.6 0.0 copy-done.3
  91.6 0.8 scatter_custom_fusion
  92.4 0.6 gather_fusion
  93.1 0.7 fusion.18
  96.9 0.0 copy-done.1
  96.9 0.6 gather_fusion.1
  98.2 0.7 fusion.17
  98.9 0.6 iota_compare_fusion
  99.5 0.6 iota_compare_fusion.1
  100.2 0.1 broadcast_and_fusion
  100.3 64.0 %all-gather.2.cloned.1.call-done = bf16[3,64,128,128]{3,2,0,1:T(8,128)(2,1)} async-done(((bf16[3,2,128,128]{3,2,0,1:T(8,128)(2,1)}), bf16[3,64,128,128]{3,2,0,1:T(8,128)(2,1)}) %all-gather.2.cloned.1.call-update) | async-done | bytes 6291472 | tf_op jit(solution)/shard_map/all_gather | solution.py:28
  164.3 1.0 dynamic-slice_select_fusion.1
  165.3 0.7 copy.14
  (8 shorter events, 0.1 us)
Async XLA Ops:
  6.5 1.0 copy-start
  6.5 3.1 %copy-start.2 = (bf16[3,48,4,4]{1,3,2,0:T(4,128)(2,1)S(1)}, bf16[3,48,4,4]{1,3,2,0:T(4,128)(2,1)}, u32[]{:S(2)}) copy-start(bf16[3,48,4,4]{1,3,2,0:T(4,128)(2,1)} %param.10) | copy-start | bytes 13828
  6.5 83.4 %reduce-scatter.2.cloned.1.call-start = ((), (), s32[]{:S(2)}) async-start(), calls=%async_computation.1 | async-start | bytes 3342336 | tf_op jit(solution)/shard_map/reduce_scatter | solution.py:27
  16.3 75.3 %copy-start.3 = (s32[64]{0:T(128)S(1)}, s32[64]{0:T(128)}, u32[]{:S(2)}) copy-start(s32[64]{0:T(128)} %param.13) | copy-start | bytes 772
  16.3 80.6 %copy-start.1 = (s32[64]{0:T(128)S(1)}, s32[64]{0:T(128)}, u32[]{:S(2)}) copy-start(s32[64]{0:T(128)} %param.12) | copy-start | bytes 772
  16.3 148.0 %all-gather.2.cloned.1.call-start = ((), (), s32[]{:S(2)}) async-start(), calls=%async_computation.2 | async-start | bytes 6488064 | tf_op jit(solution)/shard_map/all_gather | solution.py:28
Sparse Core Ops, SparseCore 0:
  16.4 73.4 reduce-scatter.1
  93.1 71.1 all-gather.1

commit v3 on v2

--- a/solution.py
+++ b/solution.py
@@ -10,9 +10,10 @@
     device = lax.axis_index("sec")
     local = jnp.arange(per_dev, dtype=jnp.int32)
     own_labels = device * per_dev + local
-    inverse = jnp.zeros((nsec,), jnp.int32).at[sector_map].set(jnp.arange(nsec, dtype=jnp.int32))
-    source = jnp.take(inverse, own_labels, axis=0)
-    sizes = jnp.take(sector_rows, source, axis=0)
+    hit = sector_map[None, :] == own_labels[:, None]
+    labels = jnp.arange(nsec, dtype=jnp.int32)
+    source = jnp.sum(jnp.where(hit, labels[None, :], 0), axis=1)
+    sizes = jnp.sum(jnp.where(hit, sector_rows[None, :], 0), axis=1)
 
     masked = jnp.where(mpo_pattern[:, :, None, None] != 0, mpo_tensor, jnp.zeros_like(mpo_tensor))
     left = jnp.einsum(

time: 173 us -> 173 us (level)
  local copies, waits for them, and re-layouts: 8.36 us -> 5.67 us
  waiting for transfers between devices: 138 us -> 140 us
    all_gather x1, waiting for transfers between devices: 64 us -> 67.1 us  [per_device(): gathered = lax.all_gather(summed, 'sec', axis=1, tiled=True)]
  transfers between devices with their start and end apart: 2 -> 2, of which waited for: 2 -> 2; matrix products, arithmetic and copies ran while one was open for 3% -> 1% of each run, Pallas kernels for 0% -> 0%
where the time goes in v3:
time: 173 us
  waiting for transfers between devices  140 us (81%)
  between operations  17.1 us (10%)
  matrix products  6.18 us (4%)
  local copies, waits for them, and re-layouts  5.67 us (3%)
  other arithmetic  3.37 us (2%)
    reduce_scatter x1, waiting for transfers between devices, per_device(): summed = lax.psum_scatter(parts, 'mpo', scatter_dimension=0, tiled=True)  73.3 us
    all_gather x1, waiting for transfers between devices, per_device(): gathered = lax.all_gather(summed, 'sec', axis=1, tiled=True)  67.1 us
    dot_general x1, matrix products, per_device(): jnp.einsum('bpst,bstgaz->pgaz', masked, sandwich, preferred_element_type=...  4.03 us
  transfers between devices with their start and end apart: 2, of which 2 were waited for; matrix products, arithmetic and copies ran while one was open for 1% of the time, Pallas kernels for 0%

profile of v3, /device:TPU:1, one launch (start us, length us, event | category | flops | bytes accessed | tf_op | source)
XLA Modules:
  0.0 172.7 jit_solution(8793652653177837608)
XLA Ops:
  6.5 0.0 copy-start
  6.5 0.0 copy-start.3
  6.5 0.0 reduce-scatter.2.cloned.1.call-start
  6.5 0.7 broadcast_compare_fusion
  7.3 0.2 copy-done
  7.5 2.1 %convert_bitcast_fusion = bf16[3,4,4,2,128,128]{5,4,2,1,0,3:T(8,128)(2,1)S(1)} fusion(bf16[2,4,128,128]{3,2,1,0:T(8,128)(2,1)S(1)} %copy-done, bf16[3,2,128,128]{3,2,1,0:T(8,128)(2,1)} %param.6), kind=kOutput, calls=%fused_computation.3 | convolution fusion | flops 505282560 | bytes 3604480 | tf_op jit(solution)/shard_map/gbsac,gtcz->bstgaz/dot_general | solution.py:22
  9.7 0.0 copy-done.3
  9.7 4.0 %bitcast_convert_fusion = bf16[48,2,128,128]{3,0,2,1:T(8,128)(2,1)S(1)} fusion(bf16[3,4,4,2,128,128]{5,4,2,1,0,3:T(8,128)(2,1)S(1)} %convert_bitcast_fusion, bf16[3,48,4,4]{1,3,2,0:T(4,128)(2,1)S(1)} %copy-done.3, pred[3,48]{1,0:T(4,128)(4,1)S(1)} %broadcast_compare_fusion), kind=kOutput, calls=%fused_computation | convolution fusion | flops 152570112 | bytes 6296208 | tf_op jit(solution)/shard_map/bpst,bstgaz->pgaz/dot_general | solution.py:25
  13.7 2.5 %copy.14 = bf16[48,2,128,128]{3,2,1,0:T(8,128)(2,1)} copy(bf16[48,2,128,128]{3,0,2,1:T(8,128)(2,1)S(1)} %bitcast_convert_fusion) | data formatting | bytes 6291456 | tf_op jit(solution)/shard_map/convert_element_type | solution.py:27
  16.2 0.0 copy-start.1
  16.2 0.0 copy-start.2
  16.2 0.0 reduce-scatter.2.cloned.1.call-update
  16.2 0.0 all-gather.2.cloned.1.call-start
  16.3 73.3 %reduce-scatter.2.cloned.1.call-done = bf16[3,2,128,128]{3,2,1,0:T(8,128)(2,1)} async-done(((bf16[48,2,128,128]{3,2,1,0:T(8,128)(2,1)}), bf16[3,2,128,128]{3,2,1,0:T(8,128)(2,1)}) %reduce-scatter.2.cloned.1.call-update) | async-done | bytes 196624 | tf_op jit(solution)/shard_map/reduce_scatter | solution.py:28
  89.6 1.6 copy.15
  91.2 0.0 all-gather.2.cloned.1.call-update
  91.2 0.0 copy-done.1
  91.2 0.0 copy-done.2
  91.3 0.2 fusion.14
  91.4 0.7 fusion.17
  95.6 0.7 iota_compare_fusion.1
  96.4 0.6 iota_compare_fusion
  97.0 0.1 broadcast_and_fusion.1
  97.1 0.1 broadcast_and_fusion
  97.2 67.1 %all-gather.2.cloned.1.call-done = bf16[3,64,128,128]{3,2,0,1:T(8,128)(2,1)} async-done(((bf16[3,2,128,128]{3,2,0,1:T(8,128)(2,1)}), bf16[3,64,128,128]{3,2,0,1:T(8,128)(2,1)}) %all-gather.2.cloned.1.call-update) | async-done | bytes 6291472 | tf_op jit(solution)/shard_map/all_gather | solution.py:29
  164.2 1.0 dynamic-slice_select_fusion.1
  165.2 0.7 copy.16
  (2 shorter events, 0.0 us)
Async XLA Ops:
  6.5 1.0 copy-start
  6.5 3.1 %copy-start.3 = (bf16[3,48,4,4]{1,3,2,0:T(4,128)(2,1)S(1)}, bf16[3,48,4,4]{1,3,2,0:T(4,128)(2,1)}, u32[]{:S(2)}) copy-start(bf16[3,48,4,4]{1,3,2,0:T(4,128)(2,1)} %param.8) | copy-start | bytes 13828
  6.5 83.0 %reduce-scatter.2.cloned.1.call-start = ((), (), s32[]{:S(2)}) async-start(), calls=%async_computation.1 | async-start | bytes 3342336 | tf_op jit(solution)/shard_map/reduce_scatter | solution.py:28
  16.2 75.1 %copy-start.1 = (s32[64]{0:T(128)S(1)}, s32[64]{0:T(128)}, u32[]{:S(2)}) copy-start(s32[64]{0:T(128)} %param.10) | copy-start | bytes 772
  16.2 75.1 %copy-start.2 = (s32[64]{0:T(128)S(1)}, s32[64]{0:T(128)}, u32[]{:S(2)}) copy-start(s32[64]{0:T(128)} %param.11) | copy-start | bytes 772
  16.2 148.0 %all-gather.2.cloned.1.call-start = ((), (), s32[]{:S(2)}) async-start(), calls=%async_computation.2 | async-start | bytes 6488064 | tf_op jit(solution)/shard_map/all_gather | solution.py:29
Sparse Core Ops, SparseCore 0:
  16.3 73.2 reduce-scatter.1
  92.7 71.4 all-gather.1

commit v4 on v3

--- a/solution.py
+++ b/solution.py
@@ -26,11 +26,16 @@
         "bpst,bstgaz->pgaz", masked, sandwich, preferred_element_type=jnp.float32
     ).astype(jnp.bfloat16)
     summed = lax.psum_scatter(parts, "mpo", scatter_dimension=0, tiled=True)
-    gathered = lax.all_gather(summed, "sec", axis=1, tiled=True)
+    summed, source, sizes = lax.optimization_barrier((summed, source, sizes))
+    gathered = lax.all_gather(summed[None], "sec", axis=0, tiled=True)
     places = jnp.arange(block, dtype=jnp.int32)
     picked = []
     for k in range(per_dev):
-        one = lax.dynamic_index_in_dim(gathered, source[k], axis=1, keepdims=False)
+        one = lax.dynamic_slice(
+            gathered,
+            (source[k] // per_dev, 0, source[k] % per_dev, 0, 0),
+            (1, channels, 1, block, block),
+        ).reshape(channels, block, block)
         keep = (places[:, None] < sizes[k]) & (places[None, :] < sizes[k])
         picked.append(jnp.where(keep[None], one, jnp.zeros_like(one)))
     return jnp.stack(picked, axis=1)

time: 173 us -> 173 us (level)
  local copies, waits for them, and re-layouts: 5.67 us -> 3.93 us
where the time goes in v4:
time: 173 us
  waiting for transfers between devices  140 us (81%)
  between operations  18.4 us (11%)
  matrix products  6.18 us (4%)
  other arithmetic  4.01 us (2%)
  local copies, waits for them, and re-layouts  3.93 us (2%)
    reduce_scatter x1, waiting for transfers between devices, per_device(): summed = lax.psum_scatter(parts, 'mpo', scatter_dimension=0, tiled=True)  72.6 us
    all_gather x1, waiting for transfers between devices, per_device(): gathered = lax.all_gather(summed[None], 'sec', axis=0, tiled=True)  67.6 us
    dot_general x1, matrix products, per_device(): jnp.einsum('bpst,bstgaz->pgaz', masked, sandwich, preferred_element_type=...  4.03 us
  transfers between devices with their start and end apart: 2, of which 2 were waited for; matrix products, arithmetic and copies ran while one was open for 1% of the time, Pallas kernels for 0%

profile of v4, /device:TPU:1, one launch (start us, length us, event | category | flops | bytes accessed | tf_op | source)
XLA Modules:
  0.0 172.7 jit_solution(13205391402576066404)
XLA Ops:
  6.5 0.0 copy-start
  6.5 0.0 copy-start.3
  6.5 0.0 reduce-scatter.2.cloned.1.call-start
  6.5 0.7 broadcast_compare_fusion
  7.3 0.2 copy-done
  7.5 2.1 %convert_bitcast_fusion = bf16[3,4,4,2,128,128]{5,4,2,1,0,3:T(8,128)(2,1)S(1)} fusion(bf16[2,4,128,128]{3,2,1,0:T(8,128)(2,1)S(1)} %copy-done, bf16[3,2,128,128]{3,2,1,0:T(8,128)(2,1)} %param.6), kind=kOutput, calls=%fused_computation.3 | convolution fusion | flops 505282560 | bytes 3604480 | tf_op jit(solution)/shard_map/gbsac,gtcz->bstgaz/dot_general | solution.py:22
  9.7 0.0 copy-done.3
  9.7 4.0 %bitcast_convert_fusion = bf16[48,2,128,128]{3,0,2,1:T(8,128)(2,1)S(1)} fusion(bf16[3,4,4,2,128,128]{5,4,2,1,0,3:T(8,128)(2,1)S(1)} %convert_bitcast_fusion, bf16[3,48,4,4]{1,3,2,0:T(4,128)(2,1)S(1)} %copy-done.3, pred[3,48]{1,0:T(4,128)(4,1)S(1)} %broadcast_compare_fusion), kind=kOutput, calls=%fused_computation | convolution fusion | flops 152570112 | bytes 6296208 | tf_op jit(solution)/shard_map/bpst,bstgaz->pgaz/dot_general | solution.py:25
  13.7 2.5 %copy.17 = bf16[48,2,128,128]{3,2,1,0:T(8,128)(2,1)} copy(bf16[48,2,128,128]{3,0,2,1:T(8,128)(2,1)S(1)} %bitcast_convert_fusion) | data formatting | bytes 6291456 | tf_op jit(solution)/shard_map/convert_element_type | solution.py:27
  16.2 0.0 copy-start.1
  16.2 0.0 copy-start.2
  16.2 0.0 reduce-scatter.2.cloned.1.call-update
  16.2 0.0 all-gather.3.cloned.1.call-start
  16.3 0.6 copy-done.1
  16.8 0.0 copy-done.2
  16.9 0.2 fusion.15
  17.0 72.6 %reduce-scatter.2.cloned.1.call-done = bf16[3,2,128,128]{3,2,1,0:T(8,128)(2,1)} async-done(((bf16[48,2,128,128]{3,2,1,0:T(8,128)(2,1)}), bf16[3,2,128,128]{3,2,1,0:T(8,128)(2,1)}) %reduce-scatter.2.cloned.1.call-update) | async-done | bytes 196624 | tf_op jit(solution)/shard_map/reduce_scatter | solution.py:28
  89.6 0.0 all-gather.3.cloned.1.call-update
  89.6 0.6 fusion.17
  95.2 0.7 iota_compare_fusion.1
  95.8 0.6 iota_compare_fusion
  96.5 0.1 broadcast_and_fusion
  96.5 0.1 broadcast_and_fusion.1
  96.6 67.6 %all-gather.3.cloned.1.call-done = bf16[96,2,128,128]{3,2,1,0:T(8,128)(2,1)} async-done(((bf16[3,2,128,128]{3,2,1,0:T(8,128)(2,1)}), bf16[96,2,128,128]{3,2,1,0:T(8,128)(2,1)}) %all-gather.3.cloned.1.call-update) | async-done | bytes 6291472 | tf_op jit(solution)/shard_map/all_gather | solution.py:30
  164.2 1.0 bitcast_select_fusion.1
  165.2 0.7 pad_maximum_fusion
  (1 shorter events, 0.0 us)
Async XLA Ops:
  6.5 1.0 copy-start
  6.5 3.1 %copy-start.3 = (bf16[3,48,4,4]{1,3,2,0:T(4,128)(2,1)S(1)}, bf16[3,48,4,4]{1,3,2,0:T(4,128)(2,1)}, u32[]{:S(2)}) copy-start(bf16[3,48,4,4]{1,3,2,0:T(4,128)(2,1)} %param.8) | copy-start | bytes 13828
  6.5 83.0 %reduce-scatter.2.cloned.1.call-start = ((), (), s32[]{:S(2)}) async-start(), calls=%async_computation.1 | async-start | bytes 3342336 | tf_op jit(solution)/shard_map/reduce_scatter | solution.py:28
  16.2 0.7 copy-start.1
  16.2 0.7 copy-start.2
  16.2 148.0 %all-gather.3.cloned.1.call-start = ((), (), s32[]{:S(2)}) async-start(), calls=%async_computation.2 | async-start | bytes 6488064 | tf_op jit(solution)/shard_map/all_gather | solution.py:30
Sparse Core Ops, SparseCore 0:
  16.3 73.2 reduce-scatter.1
  92.7 71.4 all-gather.2

commit v5 on v4

--- a/solution.py
+++ b/solution.py
@@ -13,7 +13,7 @@
     hit = sector_map[None, :] == own_labels[:, None]
     labels = jnp.arange(nsec, dtype=jnp.int32)
     source = jnp.sum(jnp.where(hit, labels[None, :], 0), axis=1)
-    sizes = jnp.sum(jnp.where(hit, sector_rows[None, :], 0), axis=1)
+    sizes = jnp.take(sector_rows, own_labels, axis=0)
 
     masked = jnp.where(mpo_pattern[:, :, None, None] != 0, mpo_tensor, jnp.zeros_like(mpo_tensor))
     left = jnp.einsum(
@@ -26,19 +26,21 @@
         "bpst,bstgaz->pgaz", masked, sandwich, preferred_element_type=jnp.float32
     ).astype(jnp.bfloat16)
     summed = lax.psum_scatter(parts, "mpo", scatter_dimension=0, tiled=True)
-    summed, source, sizes = lax.optimization_barrier((summed, source, sizes))
+    places = jnp.arange(block, dtype=jnp.int32)
+    keep = (places[None, :, None] < sizes[:, None, None]) & (
+        places[None, None, :] < sizes[:, None, None]
+    )
+    summed = jnp.where(keep[None], summed, jnp.zeros_like(summed))
     gathered = lax.all_gather(summed[None], "sec", axis=0, tiled=True)
-    places = jnp.arange(block, dtype=jnp.int32)
-    picked = []
-    for k in range(per_dev):
-        one = lax.dynamic_slice(
+    picked = [
+        lax.dynamic_slice(
             gathered,
             (source[k] // per_dev, 0, source[k] % per_dev, 0, 0),
             (1, channels, 1, block, block),
-        ).reshape(channels, block, block)
-        keep = (places[:, None] < sizes[k]) & (places[None, :] < sizes[k])
-        picked.append(jnp.where(keep[None], one, jnp.zeros_like(one)))
-    return jnp.stack(picked, axis=1)
+        )[0]
+        for k in range(per_dev)
+    ]
+    return jnp.concatenate(picked, axis=1)
 
 
 def solution(mesh):

time: 173 us -> 173 us (level)
  no operation moved by 1% of the time
where the time goes in v5:
time: 173 us
  waiting for transfers between devices  139 us (80%)
  between operations  18.2 us (11%)
  matrix products  6.18 us (4%)
  local copies, waits for them, and re-layouts  5.45 us (3%)
  other arithmetic  3.43 us (2%)
    reduce_scatter x1, waiting for transfers between devices, per_device(): summed = lax.psum_scatter(parts, 'mpo', scatter_dimension=0, tiled=True)  71.9 us
    all_gather x1, waiting for transfers between devices, per_device(): gathered = lax.all_gather(summed[None], 'sec', axis=0, tiled=True)  67.5 us
    dot_general x1, matrix products, per_device(): jnp.einsum('bpst,bstgaz->pgaz', masked, sandwich, preferred_element_type=...  4.03 us
  transfers between devices with their start and end apart: 2, of which 2 were waited for; matrix products, arithmetic and copies ran while one was open for 1% of the time, Pallas kernels for 0%

profile of v5, /device:TPU:1, one launch (start us, length us, event | category | flops | bytes accessed | tf_op | source)
XLA Modules:
  0.0 172.7 jit_solution(2927412540008155056)
XLA Ops:
  6.5 0.0 copy-start
  6.5 0.0 copy-start.2
  6.5 0.0 reduce-scatter.2.cloned.1.call-start
  6.5 0.7 broadcast_compare_fusion
  7.3 0.2 copy-done
  7.5 2.1 %convert_bitcast_fusion = bf16[3,4,4,2,128,128]{5,4,2,1,0,3:T(8,128)(2,1)S(1)} fusion(bf16[2,4,128,128]{3,2,1,0:T(8,128)(2,1)S(1)} %copy-done, bf16[3,2,128,128]{3,2,1,0:T(8,128)(2,1)} %param.6), kind=kOutput, calls=%fused_computation.4 | convolution fusion | flops 505282560 | bytes 3604480 | tf_op jit(solution)/shard_map/gbsac,gtcz->bstgaz/dot_general | solution.py:22
  9.7 0.0 copy-done.2
  9.7 4.0 %bitcast_convert_fusion = bf16[48,2,128,128]{3,0,2,1:T(8,128)(2,1)S(1)} fusion(bf16[3,4,4,2,128,128]{5,4,2,1,0,3:T(8,128)(2,1)S(1)} %convert_bitcast_fusion, bf16[3,48,4,4]{1,3,2,0:T(4,128)(2,1)S(1)} %copy-done.2, pred[3,48]{1,0:T(4,128)(4,1)S(1)} %broadcast_compare_fusion), kind=kOutput, calls=%fused_computation.1 | convolution fusion | flops 152570112 | bytes 6296208 | tf_op jit(solution)/shard_map/bpst,bstgaz->pgaz/dot_general | solution.py:25
  13.7 2.5 %copy.17 = bf16[48,2,128,128]{3,2,1,0:T(8,128)(2,1)} copy(bf16[48,2,128,128]{3,0,2,1:T(8,128)(2,1)S(1)} %bitcast_convert_fusion) | data formatting | bytes 6291456 | tf_op jit(solution)/shard_map/convert_element_type | solution.py:27
  16.2 0.0 copy-start.1
  16.2 0.0 copy-start.3
  16.2 0.0 reduce-scatter.2.cloned.1.call-update
  16.2 0.0 all-gather.3.cloned.1.call-start
  16.3 0.5 copy-done.1
  16.8 0.6 gather_fusion
  17.5 0.1 iota_compare_fusion
  17.6 0.1 broadcast_and_fusion
  17.7 71.9 %reduce-scatter.2.cloned.1.call-done = bf16[3,2,128,128]{3,2,1,0:T(8,128)(2,1)} async-done(((bf16[48,2,128,128]{3,2,1,0:T(8,128)(2,1)}), bf16[3,2,128,128]{3,2,1,0:T(8,128)(2,1)}) %reduce-scatter.2.cloned.1.call-update) | async-done | bytes 196624 | tf_op jit(solution)/shard_map/reduce_scatter | solution.py:28
  89.6 1.6 broadcast_select_fusion
  91.2 0.0 all-gather.3.cloned.1.call-update
  91.2 0.0 copy-done.3
  91.2 0.2 fusion.14
  91.4 0.6 fusion.17
  96.8 67.5 %all-gather.3.cloned.1.call-done = bf16[96,2,128,128]{3,2,1,0:T(8,128)(2,1)} async-done(((bf16[3,2,128,128]{3,2,1,0:T(8,128)(2,1)}), bf16[96,2,128,128]{3,2,1,0:T(8,128)(2,1)}) %all-gather.3.cloned.1.call-update) | async-done | bytes 6291472 | tf_op jit(solution)/shard_map/all_gather | solution.py:34
  164.2 1.0 dynamic-slice_bitcast_fusion.1
  165.2 0.7 pad_maximum_fusion
  (3 shorter events, 0.0 us)
Async XLA Ops:
  6.5 1.0 copy-start
  6.5 3.1 %copy-start.2 = (bf16[3,48,4,4]{1,3,2,0:T(4,128)(2,1)S(1)}, bf16[3,48,4,4]{1,3,2,0:T(4,128)(2,1)}, u32[]{:S(2)}) copy-start(bf16[3,48,4,4]{1,3,2,0:T(4,128)(2,1)} %param.8) | copy-start | bytes 13828
  6.5 83.0 %reduce-scatter.2.cloned.1.call-start = ((), (), s32[]{:S(2)}) async-start(), calls=%async_computation.1 | async-start | bytes 3342336 | tf_op jit(solution)/shard_map/reduce_scatter | solution.py:28
  16.2 0.7 copy-start.1
  16.2 75.0 %copy-start.3 = (s32[64]{0:T(128)S(1)}, s32[64]{0:T(128)}, u32[]{:S(2)}) copy-start(s32[64]{0:T(128)} %param.11) | copy-start | bytes 772
  16.2 148.0 %all-gather.3.cloned.1.call-start = ((), (), s32[]{:S(2)}) async-start(), calls=%async_computation.2 | async-start | bytes 6488064 | tf_op jit(solution)/shard_map/all_gather | solution.py:34
Sparse Core Ops, SparseCore 0:
  16.3 73.2 reduce-scatter.1
  92.7 71.4 all-gather.2

commit v6 on v3

--- a/solution.py
+++ b/solution.py
@@ -15,7 +15,7 @@
     source = jnp.sum(jnp.where(hit, labels[None, :], 0), axis=1)
     sizes = jnp.sum(jnp.where(hit, sector_rows[None, :], 0), axis=1)
 
-    masked = jnp.where(mpo_pattern[:, :, None, None] != 0, mpo_tensor, jnp.zeros_like(mpo_tensor))
+    masked = mpo_tensor * mpo_pattern.astype(mpo_tensor.dtype)[:, :, None, None]
     left = jnp.einsum(
         "gsxa,bgxc->gbsac", site_tensor, environment, preferred_element_type=jnp.float32
     ).astype(jnp.bfloat16)

time: 173 us -> 173 us (level)
  no operation moved by 1% of the time
where the time goes in v6:
time: 173 us
  waiting for transfers between devices  140 us (81%)
  between operations  17.1 us (10%)
  matrix products  6.17 us (4%)
  local copies, waits for them, and re-layouts  5.67 us (3%)
  other arithmetic  3.37 us (2%)
    reduce_scatter x1, waiting for transfers between devices, per_device(): summed = lax.psum_scatter(parts, 'mpo', scatter_dimension=0, tiled=True)  72.6 us
    all_gather x1, waiting for transfers between devices, per_device(): gathered = lax.all_gather(summed, 'sec', axis=1, tiled=True)  67.7 us
    dot_general x1, matrix products, per_device(): jnp.einsum('bpst,bstgaz->pgaz', masked, sandwich, preferred_element_type=...  4.03 us
  transfers between devices with their start and end apart: 2, of which 2 were waited for; matrix products, arithmetic and copies ran while one was open for 1% of the time, Pallas kernels for 0%

profile of v6, /device:TPU:1, one launch (start us, length us, event | category | flops | bytes accessed | tf_op | source)
XLA Modules:
  0.0 172.7 jit_solution(248844029406936744)
XLA Ops:
  6.5 0.0 copy-start
  6.5 0.0 copy-start.3
  6.5 0.0 reduce-scatter.2.cloned.1.call-start
  6.5 0.7 convert_element_type.18
  7.3 0.2 copy-done
  7.5 2.1 %convert_bitcast_fusion = bf16[3,4,4,2,128,128]{5,4,2,1,0,3:T(8,128)(2,1)S(1)} fusion(bf16[2,4,128,128]{3,2,1,0:T(8,128)(2,1)S(1)} %copy-done, bf16[3,2,128,128]{3,2,1,0:T(8,128)(2,1)} %param.6), kind=kOutput, calls=%fused_computation.3 | convolution fusion | flops 505282560 | bytes 3604480 | tf_op jit(solution)/shard_map/gbsac,gtcz->bstgaz/dot_general | solution.py:22
  9.7 0.0 copy-done.3
  9.7 4.0 %bitcast_convert_fusion = bf16[48,2,128,128]{3,0,2,1:T(8,128)(2,1)S(1)} fusion(bf16[3,4,4,2,128,128]{5,4,2,1,0,3:T(8,128)(2,1)S(1)} %convert_bitcast_fusion, bf16[3,48,4,4]{1,3,2,0:T(4,128)(2,1)S(1)} %copy-done.3, bf16[3,48]{1,0:T(4,128)(2,1)S(1)} %convert_element_type.18), kind=kOutput, calls=%fused_computation | convolution fusion | flops 152577024 | bytes 6296352 | tf_op jit(solution)/shard_map/bpst,bstgaz->pgaz/dot_general | solution.py:25
  13.7 2.5 %copy.14 = bf16[48,2,128,128]{3,2,1,0:T(8,128)(2,1)} copy(bf16[48,2,128,128]{3,0,2,1:T(8,128)(2,1)S(1)} %bitcast_convert_fusion) | data formatting | bytes 6291456 | tf_op jit(solution)/shard_map/convert_element_type | solution.py:27
  16.2 0.0 copy-start.1
  16.2 0.0 copy-start.2
  16.2 0.0 reduce-scatter.2.cloned.1.call-update
  16.2 0.0 all-gather.2.cloned.1.call-start
  16.2 72.6 %reduce-scatter.2.cloned.1.call-done = bf16[3,2,128,128]{3,2,1,0:T(8,128)(2,1)} async-done(((bf16[48,2,128,128]{3,2,1,0:T(8,128)(2,1)}), bf16[3,2,128,128]{3,2,1,0:T(8,128)(2,1)}) %reduce-scatter.2.cloned.1.call-update) | async-done | bytes 196624 | tf_op jit(solution)/shard_map/reduce_scatter | solution.py:28
  88.9 1.6 copy.15
  90.5 0.0 all-gather.2.cloned.1.call-update
  90.5 0.0 copy-done.1
  90.5 0.0 copy-done.2
  90.6 0.2 fusion.13
  90.7 0.7 fusion.15
  94.9 0.7 iota_compare_fusion.1
  95.6 0.6 iota_compare_fusion
  96.3 0.1 broadcast_and_fusion.1
  96.4 0.1 broadcast_and_fusion
  96.5 67.7 %all-gather.2.cloned.1.call-done = bf16[3,64,128,128]{3,2,0,1:T(8,128)(2,1)} async-done(((bf16[3,2,128,128]{3,2,0,1:T(8,128)(2,1)}), bf16[3,64,128,128]{3,2,0,1:T(8,128)(2,1)}) %all-gather.2.cloned.1.call-update) | async-done | bytes 6291472 | tf_op jit(solution)/shard_map/all_gather | solution.py:29
  164.2 1.0 dynamic-slice_select_fusion.1
  165.2 0.7 copy.16
  (2 shorter events, 0.0 us)
Async XLA Ops:
  6.5 1.0 copy-start
  6.5 3.1 %copy-start.3 = (bf16[3,48,4,4]{1,3,2,0:T(4,128)(2,1)S(1)}, bf16[3,48,4,4]{1,3,2,0:T(4,128)(2,1)}, u32[]{:S(2)}) copy-start(bf16[3,48,4,4]{1,3,2,0:T(4,128)(2,1)} %param.8) | copy-start | bytes 13828
  6.5 82.3 %reduce-scatter.2.cloned.1.call-start = ((), (), s32[]{:S(2)}) async-start(), calls=%async_computation.1 | async-start | bytes 3342336 | tf_op jit(solution)/shard_map/reduce_scatter | solution.py:28
  16.2 74.4 %copy-start.1 = (s32[64]{0:T(128)S(1)}, s32[64]{0:T(128)}, u32[]{:S(2)}) copy-start(s32[64]{0:T(128)} %param.10) | copy-start | bytes 772
  16.2 74.4 %copy-start.2 = (s32[64]{0:T(128)S(1)}, s32[64]{0:T(128)}, u32[]{:S(2)}) copy-start(s32[64]{0:T(128)} %param.11) | copy-start | bytes 772
  16.2 148.0 %all-gather.2.cloned.1.call-start = ((), (), s32[]{:S(2)}) async-start(), calls=%async_computation.2 | async-start | bytes 6488064 | tf_op jit(solution)/shard_map/all_gather | solution.py:29
Sparse Core Ops, SparseCore 0:
  16.3 72.5 reduce-scatter.1
  92.0 72.1 all-gather.1
